TPU v7x, 32 devices: a whole 2x2x4 slice. The times are simulated.
32 devices in a mesh: dp: 2 (over core), expert: 16 (over z, y, x).
Axes of the slice: x: 2, y: 2, z: 4, core: 2. Of those that a mesh axis runs over, the one named last changes fastest.
Arguments:
- tokens: bfloat16 [1024, 3584], P(('dp', 'expert')), may hold values from -6 to 6
- out_grad: bfloat16 [1024, 3584], P(('dp', 'expert')), may hold values from -6 to 6
- expert_ids: int32 [1024, 8], P(('dp', 'expert')), may hold values from 0 to 15, all different within a row; in each aligned block of 32 rows (0 to 31, 32 to 63, ...) at most 20 rows name the same one
- gate_probs: float32 [1024, 8], P(('dp', 'expert')), may hold values from 0.2 to 1.5
- weights: bfloat16 [16, 3584, 3, 128], P('expert', 'dp'), may hold values from -0.09375 to 0.09375
- first_moment: bfloat16 [16, 3584, 3, 128], P('expert', 'dp'), may hold values from -6 to 6
- second_moment: bfloat16 [16, 3584, 3, 128], P('expert', 'dp'), may hold values from 0.5 to 5
- moving_pairs: int32 [8], replicated, may hold values from 0 to 1, as said below
Outputs:
- token_grad: bfloat16 [1024, 3584], P(('dp', 'expert'))
- prob_grad: bfloat16 [1024, 8], P(('dp', 'expert'))
- moved_weights: bfloat16 [16, 3584, 3, 128], P('expert', 'dp')
- weight_grad: float32 [16, 3584, 3, 128], P('expert', 'dp')
- new_first: bfloat16 [16, 3584, 3, 128], P('expert', 'dp')
- new_second: bfloat16 [16, 3584, 3, 128], P('expert', 'dp')
Inputs may be any that keep to these rules, and one draw needn't show every extreme that they name: `expert_ids`: each row names 8 different experts. Among the entries of the 32 rows of one device, no expert is named more than 20 times, a bound that some block reaches. `moving_pairs`: entry p is 1 where devices p and p + 8 of the expert axis exchange their experts. The last entry is always 1.
All inputs are finite; a program needn't handle non-finite values.
Results may differ from a plain program's by a relative error of at most 0.018.
Values may be sent and summed in bfloat16 or wider, within the bound.
No kernel may reach another device: no remote copies, remote signals or barrier semaphores. Data moves between devices by JAX's collectives and lax.ppermute only.
A program may use at most 64 MiB of HBM per device.

v0:
```python
import jax
import jax.numpy as jnp
from jax import lax
from jax.sharding import PartitionSpec as P


def from_partner(value, axis, bit):
    return lax.ppermute(value, axis, [(i, i ^ 1 << bit) for i in range(lax.axis_size(axis))])


def silu_parts(pre_gate):
    sig = jax.nn.sigmoid(pre_gate)
    return (pre_gate * sig, sig * (1.0 + pre_gate * (1.0 - sig)))


def on_device(
    tokens, out_grad, expert_ids, gate_probs, weights, first_moment, second_moment, moving_pairs
):
    axis_width = lax.axis_size("expert")
    half_axis = axis_width // 2
    swap_bit = half_axis.bit_length() - 1
    groups = lax.axis_size("dp")
    my_index = lax.axis_index("expert")
    tok_rows, route_count = expert_ids.shape
    model_width = tokens.shape[1]
    entry_count = tok_rows * route_count
    slot_cap = 5 * entry_count // (4 * axis_width)
    slot_count = axis_width * slot_cap
    pair_lanes = jnp.arange(half_axis, dtype=jnp.int32)
    my_move = jnp.sum(jnp.where(pair_lanes == my_index % half_axis, moving_pairs, 0))
    swapped = my_move == 1
    flat_ids = expert_ids.reshape(-1)
    theirs = from_partner((weights, first_moment, second_moment), "expert", swap_bit)
    weights = jnp.where(swapped, theirs[0], weights)
    first_moment = jnp.where(swapped, theirs[1], first_moment)
    second_moment = jnp.where(swapped, theirs[2], second_moment)
    lane_hit = (flat_ids % half_axis)[:, None] == pair_lanes[None, :]
    moves = jnp.sum(jnp.where(lane_hit, moving_pairs[None, :], 0), axis=1)
    target_dev = jnp.where(moves == 1, (flat_ids + half_axis) % axis_width, flat_ids)
    id_onehot = (flat_ids[:, None] == jnp.arange(axis_width, dtype=jnp.int32)[None, :]).astype(
        jnp.int32
    )
    id_rank = jnp.sum((jnp.cumsum(id_onehot, axis=0) - id_onehot) * id_onehot, axis=1)
    slot_of = target_dev * slot_cap + id_rank
    slot_hit = jnp.arange(slot_count, dtype=jnp.int32)[:, None] == slot_of[None, :]
    filled = jnp.any(slot_hit, axis=1)
    entry_lanes = jnp.arange(entry_count, dtype=jnp.int32)
    slot_entry = jnp.sum(jnp.where(slot_hit, entry_lanes[None, :], 0), axis=1)
    token_of = slot_entry // route_count
    flat_gate = gate_probs.reshape(-1)
    zero_row = jnp.zeros((), jnp.bfloat16)
    send_rows = jnp.where(filled[:, None], tokens[token_of], zero_row).reshape(
        axis_width, slot_cap, model_width
    )
    send_grads = jnp.where(filled[:, None], out_grad[token_of], zero_row).reshape(
        axis_width, slot_cap, model_width
    )
    send_gate = (
        jnp.where(filled, flat_gate[slot_entry], 0.0)
        .astype(jnp.bfloat16)
        .reshape(axis_width, slot_cap)
    )
    recv_rows, recv_grads, recv_gate = (
        lax.all_to_all(send_rows, "expert", split_axis=0, concat_axis=0, tiled=True),
        lax.all_to_all(send_grads, "expert", split_axis=0, concat_axis=0, tiled=True),
        lax.all_to_all(send_gate, "expert", split_axis=0, concat_axis=0, tiled=True),
    )
    whole = lax.all_gather(weights, "dp", axis=1, tiled=True)[0]
    w_gate = whole[:, 0, :]
    w_up = whole[:, 1, :]
    w_down = whole[:, 2, :]
    w_both = jnp.concatenate([w_gate, w_up], axis=1)
    rows = recv_rows.reshape(slot_count, model_width)
    pre_gate = jnp.dot(rows, w_gate, preferred_element_type=jnp.float32)
    pre_up = jnp.dot(rows, w_up, preferred_element_type=jnp.float32)
    activated, act_slope = silu_parts(pre_gate)
    hidden = (activated * pre_up).astype(jnp.bfloat16)
    contract_hidden = (((1,), (1,)), ((), ()))
    grads_in = recv_grads.reshape(slot_count, model_width)
    gates = recv_gate.reshape(slot_count).astype(jnp.float32)
    projected = jnp.dot(grads_in, w_down, preferred_element_type=jnp.float32)
    gate_rows = jnp.sum(hidden.astype(jnp.float32) * projected, axis=1).astype(jnp.bfloat16)
    scaled_grad = (gates[:, None] * grads_in.astype(jnp.float32)).astype(jnp.bfloat16)
    hidden_grad = jnp.dot(scaled_grad, w_down, preferred_element_type=jnp.float32)
    gate_delta = (hidden_grad * pre_up * act_slope).astype(jnp.bfloat16)
    up_delta = (hidden_grad * activated).astype(jnp.bfloat16)
    both_delta = jnp.concatenate([gate_delta, up_delta], axis=1)
    row_grad = lax.dot_general(
        both_delta, w_both, contract_hidden, preferred_element_type=jnp.float32
    )
    row_grad = row_grad.astype(jnp.bfloat16)
    back_rows, back_gate = (
        lax.all_to_all(
            row_grad.reshape(axis_width, slot_cap, model_width),
            "expert",
            split_axis=0,
            concat_axis=0,
            tiled=True,
        ),
        lax.all_to_all(
            gate_rows.reshape(axis_width, slot_cap),
            "expert",
            split_axis=0,
            concat_axis=0,
            tiled=True,
        ),
    )
    contract_rows = (((0,), (0,)), ((), ()))
    grad_gate = lax.dot_general(rows, gate_delta, contract_rows, preferred_element_type=jnp.float32)
    grad_up = lax.dot_general(rows, up_delta, contract_rows, preferred_element_type=jnp.float32)
    grad_down = lax.dot_general(
        scaled_grad, hidden, contract_rows, preferred_element_type=jnp.float32
    )
    grad = lax.psum_scatter(
        jnp.stack([grad_gate, grad_up, grad_down], axis=1).astype(jnp.bfloat16),
        "dp",
        scatter_dimension=0,
        tiled=True,
    ).astype(jnp.float32) * (1.0 / groups)
    grad = grad[None]
    new_first = (0.9 * first_moment.astype(jnp.float32) + 0.1 * grad).astype(jnp.bfloat16)
    new_second = (0.95 * second_moment.astype(jnp.float32) + 0.05 * grad * grad).astype(
        jnp.bfloat16
    )
    gathered = back_rows.reshape(slot_count, model_width)[slot_of].astype(jnp.float32)
    token_grad = (
        (gathered * flat_gate[:, None])
        .reshape(tok_rows, route_count, model_width)
        .sum(axis=1)
        .astype(jnp.bfloat16)
    )
    prob_grad = back_gate.reshape(slot_count)[slot_of].reshape(tok_rows, route_count)
    return (token_grad, prob_grad, weights, grad, new_first, new_second)


def solution(mesh):
    in_specs = (
        P(("dp", "expert"), None),
        P(("dp", "expert"), None),
        P(("dp", "expert"), None),
        P(("dp", "expert"), None),
        P("expert", "dp", None, None),
        P("expert", "dp", None, None),
        P("expert", "dp", None, None),
        P(),
    )
    out_specs = (
        P(("dp", "expert"), None),
        P(("dp", "expert"), None),
        P("expert", "dp", None, None),
        P("expert", "dp", None, None),
        P("expert", "dp", None, None),
        P("expert", "dp", None, None),
    )
    return jax.shard_map(
        on_device, mesh=mesh, in_specs=in_specs, out_specs=out_specs, check_vma=False
    )
```

profile of v0, /device:TPU:0, one launch (start us, length us, event | category | flops | bytes accessed | tf_op | source)
XLA Modules:
  0.0 456.9 jit_solution(9229121527226329171)
XLA Ops:
  7.2 0.8 copy.39
  8.0 0.1 reshape.341
  8.1 0.1 eq.92
  8.2 0.6 reduce-window.6
  8.8 0.2 slice_reduce_fusion
  9.0 0.1 fusion.25
  9.1 0.7 select_reduce_fusion.1
  9.9 0.1 select_reduce_fusion
  10.0 0.2 fusion.18
  10.2 0.8 copy.42
  11.0 0.1 reshape.343
  11.1 2.4 gather_fusion
  13.4 0.7 convert_element_type.137
  14.1 8.3 %all-to-all-start = ((bf16[16,1,20]{2,1,0:T(2,128)(2,1)}), bf16[16,1,20]{2,1,0:T(2,128)(2,1)S(1)}, u32[]{:S(2)}, u32[]{:S(2)}) async-start(bf16[16,1,20]{2,1,0:T(2,128)(2,1)} %convert_element_type.137), calls=%async_computation | async-start | bytes 16384 | tf_op jit(solution)/shard_map/all_to_all | solution.py:66
  22.5 0.1 broadcast_in_dim.73
  22.6 3.7 gather_fusion.1
  26.3 2.6 gather.21
  28.9 3.7 gather_fusion.2
  32.6 4.1 gather.23
  36.7 4.7 %broadcast_select_fusion = (bf16[16,20,3584]{2,1,0:T(8,128)(2,1)}, bf16[16,20,3584]{2,1,0:T(8,128)(2,1)}) fusion(bf16[16,20,3584]{2,1,0:T(8,128)(2,1)} %gather.23, pred[16,20]{1,0:T(8,128)(4,1)S(1)} %broadcast_in_dim.73, bf16[16,20,3584]{2,1,0:T(8,128)(2,1)S(1)} %gather.21), kind=kLoop, calls=%fused_computation.28 | loop fusion | flops 2293760 | bytes 9175360 | tf_op jit(solution)/shard_map/jit(_where)/select_n | solution.py:52
  41.4 6.9 %all-to-all-start.1 = ((bf16[16,20,3584]{2,1,0:T(8,128)(2,1)}), bf16[16,20,3584]{2,1,0:T(8,128)(2,1)S(1)}, u32[]{:S(2)}, u32[]{:S(2)}) async-start(bf16[16,20,3584]{2,1,0:T(8,128)(2,1)} %get-tuple-element.42), calls=%async_computation.1 | async-start | bytes 5505024 | tf_op jit(solution)/shard_map/all_to_all | solution.py:65
  48.3 2.8 collective-permute-start
  51.2 80.3 %all-to-all-done.1 = bf16[16,20,3584]{2,1,0:T(8,128)(2,1)S(1)} async-done(((bf16[16,20,3584]{2,1,0:T(8,128)(2,1)}), bf16[16,20,3584]{2,1,0:T(8,128)(2,1)S(1)}, u32[]{:S(2)}, u32[]{:S(2)}) %all-to-all-start.1) | async-done | bytes 2293792 | tf_op jit(solution)/shard_map/all_to_all | solution.py:65
  131.5 14.8 %all-to-all-start.2 = ((bf16[16,20,3584]{2,1,0:T(8,128)(2,1)}), bf16[16,20,3584]{2,1,0:T(8,128)(2,1)}, u32[]{:S(2)}, u32[]{:S(2)}) async-start(bf16[16,20,3584]{2,1,0:T(8,128)(2,1)} %get-tuple-element.41), calls=%async_computation.2 | async-start | bytes 5505024 | tf_op jit(solution)/shard_map/all_to_all | solution.py:64
  146.4 0.6 fusion.33
  147.7 52.0 %collective-permute-done = bf16[1,1792,3,128]{3,1,2,0:T(8,128)(2,1)} collective-permute-done((bf16[1,1792,3,128]{3,1,2,0:T(8,128)(2,1)}, bf16[1,1792,3,128]{3,1,2,0:T(8,128)(2,1)}, u32[]{:S(2)}, u32[]{:S(2)}) %collective-permute-start) | collective-permute-done | bytes 1376288 | tf_op jit(solution)/shard_map/ppermute | solution.py:8
  199.7 2.6 broadcast_select_fusion.2
  202.3 0.2 reduce-scatter.2.cloned.1.call-start
  202.7 2.4 multiply_convert_fusion
  205.1 2.7 convert_element_type.114
  207.8 6.0 %all-gather.2.cloned.1.call-done = bf16[1,3584,3,128]{3,1,2,0:T(8,128)(2,1)} async-done(((bf16[1,1792,3,128]{3,1,2,0:T(8,128)(2,1)}), bf16[1,3584,3,128]{3,1,2,0:T(8,128)(2,1)}) %all-gather.2.cloned.1.call-update) | async-done | bytes 2752528 | tf_op jit(solution)/shard_map/all_gather | solution.py:68
  213.9 1.9 fusion.17
  215.8 4.3 all-to-all-done.2
  220.1 2.7 reshape.344
  222.8 1.9 fusion.36
  224.7 2.6 multiply_convert_fusion.3
  227.3 0.9 fusion
  228.3 1.9 fusion.1
  230.1 2.7 reshape.348
  232.9 2.1 fusion.2
  234.9 1.9 pad_maximum_fusion
  236.8 2.5 slice_bitcast_fusion
  239.4 2.0 fusion.16
  241.4 0.7 convert_element_type.138
  242.1 12.8 %all-to-all-start.4 = ((bf16[16,1,20]{2,1,0:T(2,128)(2,1)}), bf16[16,1,20]{2,1,0:T(2,128)(2,1)S(1)}, u32[]{:S(2)}, u32[]{:S(2)}) async-start(bf16[16,1,20]{2,1,0:T(2,128)(2,1)} %convert_element_type.138), calls=%async_computation.4 | async-start | bytes 16384 | tf_op jit(solution)/shard_map/all_to_all | solution.py:100
  254.9 2.0 convolution_convert_fusion
  256.9 2.2 reshape.345
  259.1 3.0 all-to-all-done.4
  262.1 4.7 %all-to-all-start.3 = ((bf16[16,20,3584]{2,1,0:T(8,128)(2,1)}), bf16[16,20,3584]{2,1,0:T(8,128)(2,1)}, u32[]{:S(2)}, u32[]{:S(2)}) async-start(bf16[16,20,3584]{2,1,0:T(8,128)(2,1)} %reshape.345), calls=%async_computation.3 | async-start | bytes 5505024 | tf_op jit(solution)/shard_map/all_to_all | solution.py:93
  266.8 2.5 collective-permute-start.1
  269.4 0.5 collective-permute-start.2
  269.8 0.1 reshape.347
  270.0 0.1 reshape.349
  270.1 1.9 gather_fusion.4
  272.0 0.1 reshape.350
  272.1 0.7 copy.47
  272.8 105.2 %all-to-all-done.3 = bf16[16,20,3584]{2,1,0:T(8,128)(2,1)} async-done(((bf16[16,20,3584]{2,1,0:T(8,128)(2,1)}), bf16[16,20,3584]{2,1,0:T(8,128)(2,1)}, u32[]{:S(2)}, u32[]{:S(2)}) %all-to-all-start.3) | async-done | bytes 2293792 | tf_op jit(solution)/shard_map/all_to_all | solution.py:93
  378.0 2.7 reshape.346
  380.7 2.9 gather_fusion.3
  383.7 3.6 fusion.3
  387.3 3.2 fusion.5
  390.5 26.3 %collective-permute-done.1 = bf16[1,1792,3,128]{3,1,2,0:T(8,128)(2,1)} collective-permute-done((bf16[1,1792,3,128]{3,1,2,0:T(8,128)(2,1)}, bf16[1,1792,3,128]{3,1,2,0:T(8,128)(2,1)}, u32[]{:S(2)}, u32[]{:S(2)}) %collective-permute-start.1) | collective-permute-done | bytes 1376288 | tf_op jit(solution)/shard_map/ppermute | solution.py:8
  416.8 28.4 %collective-permute-done.2 = bf16[1,1792,3,128]{3,1,2,0:T(8,128)(2,1)} collective-permute-done((bf16[1,1792,3,128]{3,1,2,0:T(8,128)(2,1)}, bf16[1,1792,3,128]{3,1,2,0:T(8,128)(2,1)}, u32[]{:S(2)}, u32[]{:S(2)}) %collective-permute-start.2) | collective-permute-done | bytes 1376288 | tf_op jit(solution)/shard_map/ppermute | solution.py:8
  445.3 4.8 %fusion.8 = (bf16[1,1792,3,128]{3,1,2,0:T(8,128)(2,1)}, bf16[1,1792,3,128]{3,1,2,0:T(8,128)(2,1)}) fusion(bf16[1792,3,128]{2,0,1:T(8,128)(2,1)S(1)} %copy-done.4, bf16[1,1792,3,128]{3,1,2,0:T(8,128)(2,1)} %collective-permute-done.2, bf16[1,1792,3,128]{3,1,2,0:T(8,128)(2,1)} %param.14, pred[]{:T(512)S(6)} %eq.100, ...), kind=kLoop, calls=%fused_computation.23 | loop fusion | flops 10321920 | bytes 9633793 | tf_op jit(solution)/shard_map/convert_element_type | solution.py:122
  (35 shorter events, 0.4 us)
Async XLA Ops:
  7.2 15.4 %copy-start = (bf16[32,3584]{1,0:T(8,128)(2,1)S(1)}, bf16[32,3584]{1,0:T(8,128)(2,1)}, u32[]{:S(2)}) copy-start(bf16[32,3584]{1,0:T(8,128)(2,1)} %param.9) | copy-start | bytes 688132
  14.1 27.3 %all-to-all-start = ((bf16[16,1,20]{2,1,0:T(2,128)(2,1)}), bf16[16,1,20]{2,1,0:T(2,128)(2,1)S(1)}, u32[]{:S(2)}, u32[]{:S(2)}) async-start(bf16[16,1,20]{2,1,0:T(2,128)(2,1)} %convert_element_type.137), calls=%async_computation | async-start | bytes 16384 | tf_op jit(solution)/shard_map/all_to_all | solution.py:66
  26.3 2.6 copy-start.2
  41.4 90.0 %all-to-all-start.1 = ((bf16[16,20,3584]{2,1,0:T(8,128)(2,1)}), bf16[16,20,3584]{2,1,0:T(8,128)(2,1)S(1)}, u32[]{:S(2)}, u32[]{:S(2)}) async-start(bf16[16,20,3584]{2,1,0:T(8,128)(2,1)} %get-tuple-element.42), calls=%async_computation.1 | async-start | bytes 5505024 | tf_op jit(solution)/shard_map/all_to_all | solution.py:65
  48.3 151.4 %collective-permute-start = (bf16[1,1792,3,128]{3,1,2,0:T(8,128)(2,1)}, bf16[1,1792,3,128]{3,1,2,0:T(8,128)(2,1)}, u32[]{:S(2)}, u32[]{:S(2)}) collective-permute-start(bf16[1,1792,3,128]{3,1,2,0:T(8,128)(2,1)} %param.12), channel_id=1, source_target_pairs={{0,8},{1,9},{2,10},{3,11},{4,12},{5,13},{6,14},{7,15},{8,0},{9,1},... | collective-permute-start | bytes 4128776 | tf_op jit(solution)/shard_map/ppermute | solution.py:8
  131.5 71.2 %copy-start.3 = (bf16[16,20,3584]{2,1,0:T(8,128)(2,1)}, bf16[16,20,3584]{2,1,0:T(8,128)(2,1)S(1)}, u32[]{:S(2)}) copy-start(bf16[16,20,3584]{2,1,0:T(8,128)(2,1)S(1)} %all-to-all-done.1) | copy-start | bytes 6881284
  131.5 14.9 %copy-start.6 = (s32[8]{0:T(128)S(1)}, s32[8]{0:T(128)}, u32[]{:S(2)}) copy-start(s32[8]{0:T(128)} %param.15) | copy-start | bytes 100
  131.5 88.6 %all-to-all-start.2 = ((bf16[16,20,3584]{2,1,0:T(8,128)(2,1)}), bf16[16,20,3584]{2,1,0:T(8,128)(2,1)}, u32[]{:S(2)}, u32[]{:S(2)}) async-start(bf16[16,20,3584]{2,1,0:T(8,128)(2,1)} %get-tuple-element.41), calls=%async_computation.2 | async-start | bytes 5505024 | tf_op jit(solution)/shard_map/all_to_all | solution.py:64
  146.3 67.5 %all-gather.2.cloned.1.call-start = ((), (), s32[]{:S(2)}) async-start(), calls=%async_computation.6 | async-start | bytes 4128768 | tf_op jit(solution)/shard_map/all_gather | solution.py:68
  202.3 185.1 %reduce-scatter.2.cloned.1.call-start = ((), (), s32[]{:S(2)}) async-start(), calls=%async_computation.7 | async-start | bytes 4128768 | tf_op jit(solution)/shard_map/reduce_scatter | solution.py:114
  232.9 2.1 copy-start.5
  236.8 2.5 copy-start.7
  242.1 20.0 %all-to-all-start.4 = ((bf16[16,1,20]{2,1,0:T(2,128)(2,1)}), bf16[16,1,20]{2,1,0:T(2,128)(2,1)S(1)}, u32[]{:S(2)}, u32[]{:S(2)}) async-start(bf16[16,1,20]{2,1,0:T(2,128)(2,1)} %convert_element_type.138), calls=%async_computation.4 | async-start | bytes 16384 | tf_op jit(solution)/shard_map/all_to_all | solution.py:100
  262.1 115.9 %all-to-all-start.3 = ((bf16[16,20,3584]{2,1,0:T(8,128)(2,1)}), bf16[16,20,3584]{2,1,0:T(8,128)(2,1)}, u32[]{:S(2)}, u32[]{:S(2)}) async-start(bf16[16,20,3584]{2,1,0:T(8,128)(2,1)} %reshape.345), calls=%async_computation.3 | async-start | bytes 5505024 | tf_op jit(solution)/shard_map/all_to_all | solution.py:93
  266.8 150.0 %collective-permute-start.1 = (bf16[1,1792,3,128]{3,1,2,0:T(8,128)(2,1)}, bf16[1,1792,3,128]{3,1,2,0:T(8,128)(2,1)}, u32[]{:S(2)}, u32[]{:S(2)}) collective-permute-start(bf16[1,1792,3,128]{3,1,2,0:T(8,128)(2,1)} %param.13), channel_id=1, source_target_pairs={{0,8},{1,9},{2,10},{3,11},{4,12},{5,13},{6,14},{7,15},{8,0},{9,1},... | collective-permute-start | bytes 4128776 | tf_op jit(solution)/shard_map/ppermute | solution.py:8
  269.4 175.9 %collective-permute-start.2 = (bf16[1,1792,3,128]{3,1,2,0:T(8,128)(2,1)}, bf16[1,1792,3,128]{3,1,2,0:T(8,128)(2,1)}, u32[]{:S(2)}, u32[]{:S(2)}) collective-permute-start(bf16[1,1792,3,128]{3,1,2,0:T(8,128)(2,1)} %param.14), channel_id=1, source_target_pairs={{0,8},{1,9},{2,10},{3,11},{4,12},{5,13},{6,14},{7,15},{8,0},{9,1},... | collective-permute-start | bytes 4128776 | tf_op jit(solution)/shard_map/ppermute | solution.py:8
  387.3 57.9 %copy-start.4 = (bf16[1792,3,128]{2,0,1:T(8,128)(2,1)S(1)}, bf16[1792,3,128]{2,0,1:T(8,128)(2,1)}, u32[]{:S(2)}) copy-start(bf16[1792,3,128]{2,0,1:T(8,128)(2,1)} %reduce-scatter.2.cloned.1.call-done) | copy-start | bytes 4128772
  445.3 4.8 %copy-start.1 = (bf16[32,3584]{1,0:T(8,128)(2,1)S(1)}, bf16[32,3584]{1,0:T(8,128)(2,1)}, u32[]{:S(2)}) copy-start(bf16[32,3584]{1,0:T(8,128)(2,1)} %param.9) | copy-start | bytes 688132
Sparse Core Ops, SparseCore 0:
  202.4 11.3 all-gather.1
  236.9 17.5 reduce-scatter.1
where the time goes:
time: 458 us; the launch traced here: 457 us
  waiting for transfers between devices  306 us (67%)
  starting transfers between devices  53.7 us (12%)
  local copies, waits for them, and re-layouts  41.5 us (9%)
  other arithmetic  25.7 us (6%)
  matrix products  15.3 us (3%)
  between operations  15 us (3%)
    ppermute x3, waiting for transfers between devices, from_partner(): lax.ppermute(value, axis, [(i, i ^ 1 << bit) for i in range(lax.axis_size...  107 us
    all_to_all x1, waiting for transfers between devices, on_device(): lax.all_to_all(row_grad.reshape(axis_width, slot_cap, model_width), 'expe...  105 us
    all_to_all x1, waiting for transfers between devices, on_device(): lax.all_to_all(send_grads, 'expert', split_axis=0, concat_axis=0, tiled=T...  80.3 us
    all_to_all x1, starting transfers between devices, on_device(): lax.all_to_all(send_rows, 'expert', split_axis=0, concat_axis=0, tiled=True)  14.8 us
    all_to_all x1, starting transfers between devices, on_device(): lax.all_to_all(gate_rows.reshape(axis_width, slot_cap), 'expert', split_a...  12.8 us
  transfers between devices with their start and end apart: 10, of which 8 were waited for; matrix products, arithmetic and copies ran while one was open for 12% of the time, Pallas kernels for 0%

commit v1 on v0

--- a/solution.py
+++ b/solution.py
@@ -2,6 +2,29 @@
 import jax.numpy as jnp
 from jax import lax
 from jax.sharding import PartitionSpec as P
+
+
+def split_up(x, dim, peers):
+    before, after = (x.shape[:dim], x.shape[dim + 1 :])
+    return jnp.moveaxis(x.reshape(*before, peers, -1, *after), dim, 0)
+
+
+def laid_out(tiles, dim):
+    shape = list(tiles.shape[1:])
+    shape[dim] *= tiles.shape[0]
+    return jnp.moveaxis(tiles, 0, dim).reshape(shape)
+
+
+def exchange_directly(x, axis, split_dim, concat_dim):
+    devices, here = (lax.axis_size(axis), lax.axis_index(axis))
+    tiles = split_up(x, split_dim, devices)
+    out = tiles
+    for step in range(1, devices):
+        target, source = ((here + step) % devices, (here - step) % devices)
+        sent = lax.dynamic_index_in_dim(tiles, target, 0)
+        other = lax.ppermute(sent, axis, [(i, (i + step) % devices) for i in range(devices)])
+        out = lax.dynamic_update_slice_in_dim(out, other, source, axis=0)
+    return laid_out(out, concat_dim)
 
 
 def from_partner(value, axis, bit):
@@ -61,7 +84,7 @@
         .reshape(axis_width, slot_cap)
     )
     recv_rows, recv_grads, recv_gate = (
-        lax.all_to_all(send_rows, "expert", split_axis=0, concat_axis=0, tiled=True),
+        exchange_directly(send_rows, "expert", 0, 0),
         lax.all_to_all(send_grads, "expert", split_axis=0, concat_axis=0, tiled=True),
         lax.all_to_all(send_gate, "expert", split_axis=0, concat_axis=0, tiled=True),
     )

time: 458 us -> 468 us (1.022)
  waiting for transfers between devices: 306 us -> 272 us
  starting transfers between devices: 53.7 us -> 82.7 us
  local copies, waits for them, and re-layouts: 41.5 us -> 54 us
    all_to_all x1, waiting for transfers between devices: 80.3 us -> 0.01 us  [on_device(): lax.all_to_all(send_grads, 'expert', split_axis=0, concat_axis=0, tiled=T...]
    ppermute x0 -> x15, waiting for transfers between devices: none -> 62 us  [exchange_directly(): lax.ppermute(sent, axis, [(i, (i + step) % devices) for i in range(device...]
    ppermute x0 -> x15, starting transfers between devices: none -> 56 us  [exchange_directly(): lax.ppermute(sent, axis, [(i, (i + step) % devices) for i in range(device...]
    ppermute x3, waiting for transfers between devices: 107 us -> 54.5 us  [from_partner(): lax.ppermute(value, axis, [(i, i ^ 1 << bit) for i in range(lax.axis_size...]
    all_to_all x1, waiting for transfers between devices: 0.01 us -> 46.7 us  [on_device(): lax.all_to_all(send_gate, 'expert', split_axis=0, concat_axis=0, tiled=True)]
    all_to_all x1 -> x0, starting transfers between devices: 14.8 us -> none  [on_device(): lax.all_to_all(send_rows, 'expert', split_axis=0, concat_axis=0, tiled=True)]
    dynamic_update_slice x0 -> x14, local copies, waits for them, and re-layouts: none -> 9.52 us  [exchange_directly(): out = lax.dynamic_update_slice_in_dim(out, other, source, axis=0)]
    all_gather x1, waiting for transfers between devices: 6.04 us -> 0.07 us  [on_device(): whole = lax.all_gather(weights, 'dp', axis=1, tiled=True)[0]]
  transfers between devices with their start and end apart: 10 -> 24, of which waited for: 8 -> 9; matrix products, arithmetic and copies ran while one was open for 12% -> 12% of each run, Pallas kernels for 0% -> 0%
where the time goes in v1:
time: 468 us; the launch traced here: 466 us
  waiting for transfers between devices  272 us (58%)
  starting transfers between devices  82.7 us (18%)
  local copies, waits for them, and re-layouts  54 us (12%)
  other arithmetic  26.3 us (6%)
  matrix products  16 us (3%)
  between operations  15.1 us (3%)
    all_to_all x1, waiting for transfers between devices, on_device(): lax.all_to_all(row_grad.reshape(axis_width, slot_cap, model_width), 'expe...  106 us
    ppermute x15, waiting for transfers between devices, exchange_directly(): lax.ppermute(sent, axis, [(i, (i + step) % devices) for i in range(device...  62 us
    ppermute x15, starting transfers between devices, exchange_directly(): lax.ppermute(sent, axis, [(i, (i + step) % devices) for i in range(device...  56 us
    ppermute x3, waiting for transfers between devices, from_partner(): lax.ppermute(value, axis, [(i, i ^ 1 << bit) for i in range(lax.axis_size...  54.5 us
    all_to_all x1, waiting for transfers between devices, on_device(): lax.all_to_all(send_gate, 'expert', split_axis=0, concat_axis=0, tiled=True)  46.7 us
    dynamic_update_slice x14, local copies, waits for them, and re-layouts, exchange_directly(): out = lax.dynamic_update_slice_in_dim(out, other, source, axis=0)  9.52 us
  transfers between devices with their start and end apart: 24, of which 9 were waited for; matrix products, arithmetic and copies ran while one was open for 12% of the time, Pallas kernels for 0%

profile of v1, /device:TPU:0, one launch (start us, length us, event | category | flops | bytes accessed | tf_op | source)
XLA Modules:
  0.0 466.5 jit_solution(7868042974689385233)
XLA Ops:
  7.2 0.8 copy.39
  9.1 0.7 select_reduce_fusion.1
  10.2 3.7 gather_fusion.2
  13.9 2.6 gather.23
  16.7 1.8 broadcast_select_fusion
  18.4 0.9 constant_dynamic-slice_fusion.14
  19.4 3.0 collective-permute-start.1
  22.4 2.6 collective-permute-start
  25.1 2.4 gather_fusion
  27.5 0.7 convert_element_type.137
  28.2 4.6 all-to-all-start
  32.8 3.7 gather_fusion.1
  36.6 2.6 gather.21
  39.2 1.8 broadcast_select_fusion.1
  40.9 2.6 constant_dynamic-slice_fusion
  43.5 1.9 collective-permute-start.2
  46.8 46.7 %all-to-all-done = bf16[16,1,20]{2,1,0:T(2,128)(2,1)S(1)} async-done(((bf16[16,1,20]{2,1,0:T(2,128)(2,1)}), bf16[16,1,20]{2,1,0:T(2,128)(2,1)S(1)}, u32[]{:S(2)}, u32[]{:S(2)}) %all-to-all-start) | async-done | bytes 672 | tf_op jit(solution)/shard_map/all_to_all | solution.py:89
  93.5 4.5 all-to-all-start.1
  98.2 2.7 collective-permute-start.3
  100.9 1.5 collective-permute-start.4
  102.4 1.5 collective-permute-start.5
  103.9 1.4 collective-permute-start.6
  106.0 46.4 %collective-permute-done.3 = bf16[1,1,20,3584]{3,2,0,1:T(8,128)(2,1)S(1)} collective-permute-done((bf16[1,1,20,3584]{3,2,0,1:T(8,128)(2,1)S(1)}, bf16[1,1,20,3584]{3,2,0,1:T(8,128)(2,1)S(1)}, u32[]{:S(2)}, u32[]{:S(2)}) %collective-permute-start.3) | collective-permute-done | bytes 143392 | tf_op jit(solution)/shard_map/ppermute | solution.py:25
  152.4 21.8 %collective-permute-start.7 = (bf16[1,1,20,3584]{3,2,0,1:T(8,128)(2,1)S(1)}, bf16[1,1,20,3584]{3,2,0,1:T(8,128)(2,1)S(1)}, u32[]{:S(2)}, u32[]{:S(2)}) collective-permute-start(bf16[1,1,20,3584]{3,2,0,1:T(8,128)(2,1)S(1)} %get-tuple-element.42), channel_id=1, source_target_pairs={{0,7},{1,8},{2,9},{3,10},{4,11},{5,12},{6,13},{7,14},{8,15},{9,0},... | collective-permute-start | bytes 430088 | tf_op jit(solution)/shard_map/ppermute | solution.py:25
  174.9 0.7 constant_dynamic-update-slice_fusion.11
  175.5 12.7 %collective-permute-done.5 = bf16[1,1,20,3584]{3,2,0,1:T(8,128)(2,1)S(1)} collective-permute-done((bf16[1,1,20,3584]{3,2,0,1:T(8,128)(2,1)S(1)}, bf16[1,1,20,3584]{3,2,0,1:T(8,128)(2,1)S(1)}, u32[]{:S(2)}, u32[]{:S(2)}) %collective-permute-start.5) | collective-permute-done | bytes 143392 | tf_op jit(solution)/shard_map/ppermute | solution.py:25
  188.9 2.8 collective-permute-done.6
  191.8 0.7 constant_dynamic-update-slice_fusion.9
  192.4 3.5 collective-permute-start.11
  196.6 10.1 %collective-permute-start.12 = (bf16[1,1,20,3584]{3,2,0,1:T(8,128)(2,1)S(1)}, bf16[1,1,20,3584]{3,2,0,1:T(8,128)(2,1)S(1)}, u32[]{:S(2)}, u32[]{:S(2)}) collective-permute-start(bf16[1,1,20,3584]{3,2,0,1:T(8,128)(2,1)S(1)} %get-tuple-element.37), channel_id=1, source_target_pairs={{0,12},{1,13},{2,14},{3,15},{4,0},{5,1},{6,2},{7,3},{8,4},{9,5},{1... | collective-permute-start | bytes 430088 | tf_op jit(solution)/shard_map/ppermute | solution.py:25
  207.4 2.6 broadcast_select_fusion.2
  210.1 6.2 %collective-permute-start.14 = (bf16[1,1,20,3584]{3,2,0,1:T(8,128)(2,1)S(1)}, bf16[1,1,20,3584]{3,2,0,1:T(8,128)(2,1)S(1)}, u32[]{:S(2)}, u32[]{:S(2)}) collective-permute-start(bf16[1,1,20,3584]{3,2,0,1:T(8,128)(2,1)S(1)} %get-tuple-element.35), channel_id=1, source_target_pairs={{0,14},{1,15},{2,0},{3,1},{4,2},{5,3},{6,4},{7,5},{8,6},{9,7},{10,... | collective-permute-start | bytes 430088 | tf_op jit(solution)/shard_map/ppermute | solution.py:25
  216.9 2.5 collective-permute-start.15
  220.1 0.7 constant_dynamic-update-slice_fusion.4
  221.4 0.7 constant_dynamic-update-slice_fusion.2
  223.5 2.9 reshape_reshape.4
  226.5 1.9 fusion.36
  228.5 4.1 multiply_convert_fusion
  232.6 4.1 convert_element_type.114
  236.7 2.6 fusion.17
  239.3 2.6 multiply_convert_fusion.3
  241.9 0.9 fusion
  242.9 1.9 fusion.1
  244.8 2.7 reshape.354
  247.5 2.1 fusion.2
  249.5 1.9 pad_maximum_fusion
  251.4 2.5 slice_bitcast_fusion
  254.0 2.0 fusion.16
  256.0 0.7 convert_element_type.138
  256.7 7.2 %all-to-all-start.3 = ((bf16[16,1,20]{2,1,0:T(2,128)(2,1)}), bf16[16,1,20]{2,1,0:T(2,128)(2,1)S(1)}, u32[]{:S(2)}, u32[]{:S(2)}) async-start(bf16[16,1,20]{2,1,0:T(2,128)(2,1)} %convert_element_type.138), calls=%async_computation.3 | async-start | bytes 16384 | tf_op jit(solution)/shard_map/all_to_all | solution.py:123
  263.9 2.0 convolution_convert_fusion
  265.9 2.2 reshape.351
  268.1 3.0 all-to-all-done.3
  271.1 4.7 %all-to-all-start.2 = ((bf16[16,20,3584]{2,1,0:T(8,128)(2,1)}), bf16[16,20,3584]{2,1,0:T(8,128)(2,1)}, u32[]{:S(2)}, u32[]{:S(2)}) async-start(bf16[16,20,3584]{2,1,0:T(8,128)(2,1)} %reshape.351), calls=%async_computation.2 | async-start | bytes 5505024 | tf_op jit(solution)/shard_map/all_to_all | solution.py:116
  275.8 2.5 collective-permute-start.16
  279.1 1.9 gather_fusion.4
  281.8 106.0 %all-to-all-done.2 = bf16[16,20,3584]{2,1,0:T(8,128)(2,1)} async-done(((bf16[16,20,3584]{2,1,0:T(8,128)(2,1)}), bf16[16,20,3584]{2,1,0:T(8,128)(2,1)}, u32[]{:S(2)}, u32[]{:S(2)}) %all-to-all-start.2) | async-done | bytes 2293792 | tf_op jit(solution)/shard_map/all_to_all | solution.py:116
  387.8 2.7 reshape.352
  390.5 2.9 gather_fusion.3
  393.5 3.6 fusion.3
  397.1 3.2 fusion.5
  400.3 26.1 %collective-permute-done.16 = bf16[1,1792,3,128]{3,1,2,0:T(8,128)(2,1)} collective-permute-done((bf16[1,1792,3,128]{3,1,2,0:T(8,128)(2,1)}, bf16[1,1792,3,128]{3,1,2,0:T(8,128)(2,1)}, u32[]{:S(2)}, u32[]{:S(2)}) %collective-permute-start.16) | collective-permute-done | bytes 1376288 | tf_op jit(solution)/shard_map/ppermute | solution.py:31
  426.4 28.4 %collective-permute-done.17 = bf16[1,1792,3,128]{3,1,2,0:T(8,128)(2,1)} collective-permute-done((bf16[1,1792,3,128]{3,1,2,0:T(8,128)(2,1)}, bf16[1,1792,3,128]{3,1,2,0:T(8,128)(2,1)}, u32[]{:S(2)}, u32[]{:S(2)}) %collective-permute-start.17) | collective-permute-done | bytes 1376288 | tf_op jit(solution)/shard_map/ppermute | solution.py:31
  454.9 4.8 %fusion.8 = (bf16[1,1792,3,128]{3,1,2,0:T(8,128)(2,1)}, bf16[1,1792,3,128]{3,1,2,0:T(8,128)(2,1)}) fusion(bf16[1792,3,128]{2,0,1:T(8,128)(2,1)S(1)} %copy-done.3, bf16[1,1792,3,128]{3,1,2,0:T(8,128)(2,1)} %collective-permute-done.17, bf16[1,1792,3,128]{3,1,2,0:T(8,128)(2,1)} %param.14, pred[]{:T(512)S(6)} %eq.130, ...), kind=kLoop, calls=%fused_computation.23 | loop fusion | flops 10321920 | bytes 9633793 | tf_op jit(solution)/shard_map/convert_element_type | solution.py:145
  (80 shorter events, 11.0 us)
Async XLA Ops:
  7.2 3.1 copy-start
  16.6 8.3 %copy-start.5 = (f32[32,8]{0,1:T(8,128)S(1)}, f32[32,8]{0,1:T(8,128)}, u32[]{:S(2)}) copy-start(f32[32,8]{0,1:T(8,128)} %param.11) | copy-start | bytes 3076
  16.6 16.2 %copy-start.2 = (bf16[32,3584]{1,0:T(8,128)(2,1)S(1)}, bf16[32,3584]{1,0:T(8,128)(2,1)}, u32[]{:S(2)}) copy-start(bf16[32,3584]{1,0:T(8,128)(2,1)} %param.9) | copy-start | bytes 688132
  19.4 21.6 %collective-permute-start.1 = (bf16[1,1,20,3584]{3,2,0,1:T(8,128)(2,1)S(1)}, bf16[1,1,20,3584]{3,2,0,1:T(8,128)(2,1)S(1)}, u32[]{:S(2)}, u32[]{:S(2)}) collective-permute-start(bf16[1,1,20,3584]{3,2,0,1:T(8,128)(2,1)S(1)} %constant_dynamic-slice_fusion.14), channel_id=1, source_target_pairs={{0,1},{1,2},{2,3},{3,4},{4,5},{5,6},{6,7},{7,8},{8,9},{9,10},{10,1... | collective-permute-start | bytes 430088 | tf_op jit(solution)/shard_map/ppermute | solution.py:25
  22.4 185.0 %collective-permute-start = (bf16[1,1792,3,128]{3,1,2,0:T(8,128)(2,1)}, bf16[1,1792,3,128]{3,1,2,0:T(8,128)(2,1)}, u32[]{:S(2)}, u32[]{:S(2)}) collective-permute-start(bf16[1,1792,3,128]{3,1,2,0:T(8,128)(2,1)} %param.12), channel_id=1, source_target_pairs={{0,8},{1,9},{2,10},{3,11},{4,12},{5,13},{6,14},{7,15},{8,0},{9,1},... | collective-permute-start | bytes 4128776 | tf_op jit(solution)/shard_map/ppermute | solution.py:31
  28.2 65.3 %all-to-all-start = ((bf16[16,1,20]{2,1,0:T(2,128)(2,1)}), bf16[16,1,20]{2,1,0:T(2,128)(2,1)S(1)}, u32[]{:S(2)}, u32[]{:S(2)}) async-start(bf16[16,1,20]{2,1,0:T(2,128)(2,1)} %convert_element_type.137), calls=%async_computation | async-start | bytes 16384 | tf_op jit(solution)/shard_map/all_to_all | solution.py:89
  40.9 4.5 copy-start.6
  43.5 60.4 %collective-permute-start.2 = (bf16[1,1,20,3584]{3,2,0,1:T(8,128)(2,1)S(1)}, bf16[1,1,20,3584]{3,2,0,1:T(8,128)(2,1)S(1)}, u32[]{:S(2)}, u32[]{:S(2)}) collective-permute-start(bf16[1,1,20,3584]{3,2,0,1:T(8,128)(2,1)S(1)} %get-tuple-element.47), channel_id=1, source_target_pairs={{0,2},{1,3},{2,4},{3,5},{4,6},{5,7},{6,8},{7,9},{8,10},{9,11},{10,... | collective-permute-start | bytes 430088 | tf_op jit(solution)/shard_map/ppermute | solution.py:25
  93.5 134.9 %all-to-all-start.1 = ((bf16[16,20,3584]{2,1,0:T(8,128)(2,1)}), bf16[16,20,3584]{2,1,0:T(8,128)(2,1)}, u32[]{:S(2)}, u32[]{:S(2)}) async-start(bf16[16,20,3584]{2,1,0:T(8,128)(2,1)} %broadcast_select_fusion.1), calls=%async_computation.1 | async-start | bytes 5505024 | tf_op jit(solution)/shard_map/all_to_all | solution.py:88
  98.0 128.5 %all-gather.2.cloned.1.call-start = ((), (), s32[]{:S(2)}) async-start(), calls=%async_computation.5 | async-start | bytes 4128768 | tf_op jit(solution)/shard_map/all_gather | solution.py:91
  98.2 54.2 %collective-permute-start.3 = (bf16[1,1,20,3584]{3,2,0,1:T(8,128)(2,1)S(1)}, bf16[1,1,20,3584]{3,2,0,1:T(8,128)(2,1)S(1)}, u32[]{:S(2)}, u32[]{:S(2)}) collective-permute-start(bf16[1,1,20,3584]{3,2,0,1:T(8,128)(2,1)S(1)} %get-tuple-element.46), channel_id=1, source_target_pairs={{0,3},{1,4},{2,5},{3,6},{4,7},{5,8},{6,9},{7,10},{8,11},{9,12},{10... | collective-permute-start | bytes 430088 | tf_op jit(solution)/shard_map/ppermute | solution.py:25
  100.9 74.0 %collective-permute-start.4 = (bf16[1,1,20,3584]{3,2,0,1:T(8,128)(2,1)S(1)}, bf16[1,1,20,3584]{3,2,0,1:T(8,128)(2,1)S(1)}, u32[]{:S(2)}, u32[]{:S(2)}) collective-permute-start(bf16[1,1,20,3584]{3,2,0,1:T(8,128)(2,1)S(1)} %get-tuple-element.45), channel_id=1, source_target_pairs={{0,4},{1,5},{2,6},{3,7},{4,8},{5,9},{6,10},{7,11},{8,12},{9,13},{1... | collective-permute-start | bytes 430088 | tf_op jit(solution)/shard_map/ppermute | solution.py:25
  102.4 85.9 %collective-permute-start.5 = (bf16[1,1,20,3584]{3,2,0,1:T(8,128)(2,1)S(1)}, bf16[1,1,20,3584]{3,2,0,1:T(8,128)(2,1)S(1)}, u32[]{:S(2)}, u32[]{:S(2)}) collective-permute-start(bf16[1,1,20,3584]{3,2,0,1:T(8,128)(2,1)S(1)} %get-tuple-element.44), channel_id=1, source_target_pairs={{0,5},{1,6},{2,7},{3,8},{4,9},{5,10},{6,11},{7,12},{8,13},{9,14},{... | collective-permute-start | bytes 430088 | tf_op jit(solution)/shard_map/ppermute | solution.py:25
  103.9 87.8 %collective-permute-start.6 = (bf16[1,1,20,3584]{3,2,0,1:T(8,128)(2,1)S(1)}, bf16[1,1,20,3584]{3,2,0,1:T(8,128)(2,1)S(1)}, u32[]{:S(2)}, u32[]{:S(2)}) collective-permute-start(bf16[1,1,20,3584]{3,2,0,1:T(8,128)(2,1)S(1)} %get-tuple-element.43), channel_id=1, source_target_pairs={{0,6},{1,7},{2,8},{3,9},{4,10},{5,11},{6,12},{7,13},{8,14},{9,15},... | collective-permute-start | bytes 430088 | tf_op jit(solution)/shard_map/ppermute | solution.py:25
  152.4 40.0 %collective-permute-start.7 = (bf16[1,1,20,3584]{3,2,0,1:T(8,128)(2,1)S(1)}, bf16[1,1,20,3584]{3,2,0,1:T(8,128)(2,1)S(1)}, u32[]{:S(2)}, u32[]{:S(2)}) collective-permute-start(bf16[1,1,20,3584]{3,2,0,1:T(8,128)(2,1)S(1)} %get-tuple-element.42), channel_id=1, source_target_pairs={{0,7},{1,8},{2,9},{3,10},{4,11},{5,12},{6,13},{7,14},{8,15},{9,0},... | collective-permute-start | bytes 430088 | tf_op jit(solution)/shard_map/ppermute | solution.py:25
  174.9 21.8 %collective-permute-start.8 = (bf16[1,1,20,3584]{3,2,0,1:T(8,128)(2,1)S(1)}, bf16[1,1,20,3584]{3,2,0,1:T(8,128)(2,1)S(1)}, u32[]{:S(2)}, u32[]{:S(2)}) collective-permute-start(bf16[1,1,20,3584]{3,2,0,1:T(8,128)(2,1)S(1)} %get-tuple-element.41), channel_id=1, source_target_pairs={{0,8},{1,9},{2,10},{3,11},{4,12},{5,13},{6,14},{7,15},{8,0},{9,1},... | collective-permute-start | bytes 430088 | tf_op jit(solution)/shard_map/ppermute | solution.py:25
  188.3 21.8 %collective-permute-start.9 = (bf16[1,1,20,3584]{3,2,0,1:T(8,128)(2,1)S(1)}, bf16[1,1,20,3584]{3,2,0,1:T(8,128)(2,1)S(1)}, u32[]{:S(2)}, u32[]{:S(2)}) collective-permute-start(bf16[1,1,20,3584]{3,2,0,1:T(8,128)(2,1)S(1)} %get-tuple-element.40), channel_id=1, source_target_pairs={{0,9},{1,10},{2,11},{3,12},{4,13},{5,14},{6,15},{7,0},{8,1},{9,2},... | collective-permute-start | bytes 430088 | tf_op jit(solution)/shard_map/ppermute | solution.py:25
  191.7 25.2 %collective-permute-start.10 = (bf16[1,1,20,3584]{3,2,0,1:T(8,128)(2,1)S(1)}, bf16[1,1,20,3584]{3,2,0,1:T(8,128)(2,1)S(1)}, u32[]{:S(2)}, u32[]{:S(2)}) collective-permute-start(bf16[1,1,20,3584]{3,2,0,1:T(8,128)(2,1)S(1)} %get-tuple-element.39), channel_id=1, source_target_pairs={{0,10},{1,11},{2,12},{3,13},{4,14},{5,15},{6,0},{7,1},{8,2},{9,3},... | collective-permute-start | bytes 430088 | tf_op jit(solution)/shard_map/ppermute | solution.py:25
  192.4 27.6 %collective-permute-start.11 = (bf16[1,1,20,3584]{3,2,0,1:T(8,128)(2,1)S(1)}, bf16[1,1,20,3584]{3,2,0,1:T(8,128)(2,1)S(1)}, u32[]{:S(2)}, u32[]{:S(2)}) collective-permute-start(bf16[1,1,20,3584]{3,2,0,1:T(8,128)(2,1)S(1)} %get-tuple-element.38), channel_id=1, source_target_pairs={{0,11},{1,12},{2,13},{3,14},{4,15},{5,0},{6,1},{7,2},{8,3},{9,4},{... | collective-permute-start | bytes 430088 | tf_op jit(solution)/shard_map/ppermute | solution.py:25
  196.6 24.1 %collective-permute-start.12 = (bf16[1,1,20,3584]{3,2,0,1:T(8,128)(2,1)S(1)}, bf16[1,1,20,3584]{3,2,0,1:T(8,128)(2,1)S(1)}, u32[]{:S(2)}, u32[]{:S(2)}) collective-permute-start(bf16[1,1,20,3584]{3,2,0,1:T(8,128)(2,1)S(1)} %get-tuple-element.37), channel_id=1, source_target_pairs={{0,12},{1,13},{2,14},{3,15},{4,0},{5,1},{6,2},{7,3},{8,4},{9,5},{1... | collective-permute-start | bytes 430088 | tf_op jit(solution)/shard_map/ppermute | solution.py:25
  207.4 14.1 %collective-permute-start.13 = (bf16[1,1,20,3584]{3,2,0,1:T(8,128)(2,1)S(1)}, bf16[1,1,20,3584]{3,2,0,1:T(8,128)(2,1)S(1)}, u32[]{:S(2)}, u32[]{:S(2)}) collective-permute-start(bf16[1,1,20,3584]{3,2,0,1:T(8,128)(2,1)S(1)} %get-tuple-element.36), channel_id=1, source_target_pairs={{0,13},{1,14},{2,15},{3,0},{4,1},{5,2},{6,3},{7,4},{8,5},{9,6},{10... | collective-permute-start | bytes 430088 | tf_op jit(solution)/shard_map/ppermute | solution.py:25
  210.0 187.1 %reduce-scatter.2.cloned.1.call-start = ((), (), s32[]{:S(2)}) async-start(), calls=%async_computation.6 | async-start | bytes 4128768 | tf_op jit(solution)/shard_map/reduce_scatter | solution.py:137
  210.1 12.1 %collective-permute-start.14 = (bf16[1,1,20,3584]{3,2,0,1:T(8,128)(2,1)S(1)}, bf16[1,1,20,3584]{3,2,0,1:T(8,128)(2,1)S(1)}, u32[]{:S(2)}, u32[]{:S(2)}) collective-permute-start(bf16[1,1,20,3584]{3,2,0,1:T(8,128)(2,1)S(1)} %get-tuple-element.35), channel_id=1, source_target_pairs={{0,14},{1,15},{2,0},{3,1},{4,2},{5,3},{6,4},{7,5},{8,6},{9,7},{10,... | collective-permute-start | bytes 430088 | tf_op jit(solution)/shard_map/ppermute | solution.py:25
  216.9 5.9 %collective-permute-start.15 = (bf16[1,1,20,3584]{3,2,0,1:T(8,128)(2,1)S(1)}, bf16[1,1,20,3584]{3,2,0,1:T(8,128)(2,1)S(1)}, u32[]{:S(2)}, u32[]{:S(2)}) collective-permute-start(bf16[1,1,20,3584]{3,2,0,1:T(8,128)(2,1)S(1)} %get-tuple-element.34), channel_id=1, source_target_pairs={{0,15},{1,0},{2,1},{3,2},{4,3},{5,4},{6,5},{7,6},{8,7},{9,8},{10,9... | collective-permute-start | bytes 430088 | tf_op jit(solution)/shard_map/ppermute | solution.py:25
  247.5 2.1 copy-start.4
  251.4 2.5 copy-start.7
  256.7 14.4 %all-to-all-start.3 = ((bf16[16,1,20]{2,1,0:T(2,128)(2,1)}), bf16[16,1,20]{2,1,0:T(2,128)(2,1)S(1)}, u32[]{:S(2)}, u32[]{:S(2)}) async-start(bf16[16,1,20]{2,1,0:T(2,128)(2,1)} %convert_element_type.138), calls=%async_computation.3 | async-start | bytes 16384 | tf_op jit(solution)/shard_map/all_to_all | solution.py:123
  271.1 116.7 %all-to-all-start.2 = ((bf16[16,20,3584]{2,1,0:T(8,128)(2,1)}), bf16[16,20,3584]{2,1,0:T(8,128)(2,1)}, u32[]{:S(2)}, u32[]{:S(2)}) async-start(bf16[16,20,3584]{2,1,0:T(8,128)(2,1)} %reshape.351), calls=%async_computation.2 | async-start | bytes 5505024 | tf_op jit(solution)/shard_map/all_to_all | solution.py:116
  275.8 150.6 %collective-permute-start.16 = (bf16[1,1792,3,128]{3,1,2,0:T(8,128)(2,1)}, bf16[1,1792,3,128]{3,1,2,0:T(8,128)(2,1)}, u32[]{:S(2)}, u32[]{:S(2)}) collective-permute-start(bf16[1,1792,3,128]{3,1,2,0:T(8,128)(2,1)} %param.13), channel_id=1, source_target_pairs={{0,8},{1,9},{2,10},{3,11},{4,12},{5,13},{6,14},{7,15},{8,0},{9,1},... | collective-permute-start | bytes 4128776 | tf_op jit(solution)/shard_map/ppermute | solution.py:31
  278.4 176.5 %collective-permute-start.17 = (bf16[1,1792,3,128]{3,1,2,0:T(8,128)(2,1)}, bf16[1,1792,3,128]{3,1,2,0:T(8,128)(2,1)}, u32[]{:S(2)}, u32[]{:S(2)}) collective-permute-start(bf16[1,1792,3,128]{3,1,2,0:T(8,128)(2,1)} %param.14), channel_id=1, source_target_pairs={{0,8},{1,9},{2,10},{3,11},{4,12},{5,13},{6,14},{7,15},{8,0},{9,1},... | collective-permute-start | bytes 4128776 | tf_op jit(solution)/shard_map/ppermute | solution.py:31
  397.1 57.7 %copy-start.3 = (bf16[1792,3,128]{2,0,1:T(8,128)(2,1)S(1)}, bf16[1792,3,128]{2,0,1:T(8,128)(2,1)}, u32[]{:S(2)}) copy-start(bf16[1792,3,128]{2,0,1:T(8,128)(2,1)} %reduce-scatter.2.cloned.1.call-done) | copy-start | bytes 4128772
  397.1 62.5 %copy-start.1 = (bf16[32,3584]{1,0:T(8,128)(2,1)S(1)}, bf16[32,3584]{1,0:T(8,128)(2,1)}, u32[]{:S(2)}) copy-start(bf16[32,3584]{1,0:T(8,128)(2,1)} %param.8) | copy-start | bytes 688132
Sparse Core Ops, SparseCore 0:
  210.1 16.3 all-gather.1
  251.6 11.9 reduce-scatter.1
